TPU v7x, 32 devices: a whole 2x2x4 slice. The times are simulated.
32 devices in a mesh: dp: 2 (over x), expert: 4 (over y, core), tensor: 4 (over z).
Axes of the slice: x: 2, y: 2, z: 4, core: 2. Of those that a mesh axis runs over, the one named last changes fastest.
Arguments:
- output_grad: bfloat16 [2048, 4096], P(('dp', 'expert'), 'tensor'), may hold values from -6 to 6
- expert_ids: int32 [2048, 2], P(('dp', 'expert')), may hold values from 0 to 3, all different within a row; in each aligned block of 256 rows (0 to 255, 256 to 511, ...) at most 192 rows name the same one
- router_weights: bfloat16 [2048, 2], P(('dp', 'expert')), may hold values from 0.099609375 to 0.8984375
- gate_preact: bfloat16 [4, 1536, 14336], P('expert', 'dp', 'tensor'), may hold values from -6 to 6
- up_preact: bfloat16 [4, 1536, 14336], P('expert', 'dp', 'tensor'), may hold values from -6 to 6
- down_weight: bfloat16 [4, 14336, 4096], P('expert', 'tensor', 'dp'), may hold values from -0.046875 to 0.046875
Outputs:
- gate_preact_grad: bfloat16 [4, 1536, 14336], P('expert', 'dp', 'tensor')
- up_preact_grad: bfloat16 [4, 1536, 14336], P('expert', 'dp', 'tensor')
- down_grad: bfloat16 [4, 14336, 4096], P('expert', 'tensor', 'dp')
- router_grad: float32 [2048, 2], P(('dp', 'expert'))
Inputs may be any that keep to these rules, and one draw needn't show every extreme that they name: `expert_ids`: the ids of one token differ. Among the 256 rows of one device no expert is named by more than 192 rows, and in every draw some expert is named by exactly 192 rows of some device.
All inputs are finite; a program needn't handle non-finite values.
Results may differ from a plain program's by a relative error of at most 0.007.
Values may be sent and summed in bfloat16 or wider, within the bound.
No kernel may reach another device: no remote copies, remote signals or barrier semaphores. Data moves between devices by JAX's collectives and lax.ppermute only.
A program may use at most 192 MiB of HBM per device.

v0:
```python
import jax
import jax.numpy as jnp
from jax import lax
from jax.sharding import PartitionSpec as P


def silu_parts(values):
    sigma = jax.nn.sigmoid(values)
    return (values * sigma, sigma * (1.0 + values * (1.0 - sigma)))


def local(output_grad, expert_ids, router_weights, gate_preact, up_preact, down_weight):
    expert_count = lax.axis_size("expert")
    tokens_here = expert_ids.shape[0]
    choices_each = expert_ids.shape[1]
    capacity = gate_preact.shape[1] // expert_count
    flat_ids = expert_ids.reshape(-1)
    one_hot = (flat_ids[:, None] == jnp.arange(expert_count, dtype=jnp.int32)).astype(jnp.int32)
    earlier = jnp.cumsum(one_hot, axis=0) - one_hot
    slot_index = jnp.sum(earlier * one_hot, axis=1)
    target = (flat_ids * capacity + slot_index).reshape(tokens_here, choices_each)
    columns = jnp.arange(expert_count * capacity, dtype=jnp.int32)
    matches = [target[:, which][:, None] == columns[None, :] for which in range(choices_each)]
    selector = jnp.zeros((tokens_here, expert_count * capacity), jnp.bfloat16)
    gate_table = jnp.zeros((tokens_here, expert_count * capacity), jnp.float32)
    for which in range(choices_each):
        selector = jnp.where(matches[which], jnp.bfloat16(1.0), selector)
        gate_table = jnp.where(
            matches[which], router_weights[:, which : which + 1].astype(jnp.float32), gate_table
        )
    gate_send = jnp.sum(gate_table, axis=0).astype(jnp.bfloat16).reshape(expert_count, capacity)
    local_weight = down_weight[0]
    gate_float = gate_preact[0].astype(jnp.float32)
    up_float = up_preact[0].astype(jnp.float32)
    active, slope = silu_parts(gate_float)
    hidden = (active * up_float).astype(jnp.bfloat16)
    contract_rows = (((0,), (0,)), ((), ()))
    contract_cols = (((1,), (1,)), ((), ()))
    whole_weight = lax.all_gather(local_weight, "dp", axis=1, tiled=True)
    outgoing = lax.dot_general(
        selector, output_grad, contract_rows, preferred_element_type=jnp.float32
    )
    outgoing = outgoing.astype(jnp.bfloat16).reshape(expert_count, capacity, -1)
    received, gate_slots = (
        lax.all_to_all(outgoing, "expert", split_axis=0, concat_axis=0, tiled=True),
        lax.all_to_all(gate_send, "expert", split_axis=0, concat_axis=0, tiled=True),
    )
    narrow_rows = received.reshape(expert_count * capacity, -1)
    gate_column = gate_slots.reshape(-1).astype(jnp.float32)[:, None]
    fragment = lax.all_gather(narrow_rows, "tensor", axis=1, tiled=True)
    upstream_sum = lax.dot_general(
        fragment, whole_weight, contract_cols, preferred_element_type=jnp.float32
    )
    scaled = (gate_column * fragment.astype(jnp.float32)).astype(jnp.bfloat16)
    grad_part = lax.dot_general(hidden, scaled, contract_rows, preferred_element_type=jnp.float32)
    grad_weight = grad_part
    upstream, grad_weight = (upstream_sum, grad_weight)
    rounded = lax.optimization_barrier(grad_weight.astype(jnp.bfloat16)).astype(jnp.float32)
    down_grad = lax.psum_scatter(
        rounded.astype(jnp.bfloat16), "dp", scatter_dimension=1, tiled=True
    )
    score = jnp.sum(hidden.astype(jnp.float32) * upstream, axis=1)
    hidden_grad = gate_column * upstream
    gate_grad = (hidden_grad * up_float * slope).astype(jnp.bfloat16)
    up_grad = (hidden_grad * active).astype(jnp.bfloat16)
    summed_scores = lax.psum(score, "tensor")
    returned = lax.all_to_all(
        summed_scores.reshape(expert_count, capacity),
        "expert",
        split_axis=0,
        concat_axis=0,
        tiled=True,
    )
    flat_scores = returned.reshape(-1)
    router_grad = jnp.stack(
        [
            jnp.sum(jnp.where(matches[which], flat_scores[None, :], 0.0), axis=1)
            for which in range(choices_each)
        ],
        axis=1,
    )
    return (gate_grad[None], up_grad[None], down_grad[None], router_grad)


def solution(mesh):
    placed = (
        P(("dp", "expert"), "tensor"),
        P(("dp", "expert"), None),
        P(("dp", "expert"), None),
        P("expert", "dp", "tensor"),
        P("expert", "dp", "tensor"),
        P("expert", "tensor", "dp"),
    )
    return jax.shard_map(
        local,
        mesh=mesh,
        in_specs=placed,
        out_specs=(
            P("expert", "dp", "tensor"),
            P("expert", "dp", "tensor"),
            P("expert", "tensor", "dp"),
            P(("dp", "expert"), None),
        ),
        check_vma=False,
    )
```

profile of v0, /device:TPU:0, one launch (start us, length us, event | category | flops | bytes accessed | tf_op | source)
XLA Modules:
  0.0 914.7 jit_solution(14753980404124492061)
XLA Ops:
  7.2 0.0 copy-start
  7.2 0.0 all-gather.4.cloned.1.call-start
  7.2 0.9 copy.28
  8.1 0.1 eq.59
  8.2 0.1 eq.55
  8.4 1.2 reduce-window.6
  9.6 0.2 slice_reduce_fusion
  9.8 0.2 reduce-window.9
  10.0 0.1 add_bitcast_fusion
  10.1 0.1 reduce_sum.48
  10.3 0.1 copy.30
  10.3 0.7 multiply_add_fusion
  11.1 0.0 copy-done
  11.1 0.8 convolution_convert_fusion.1
  11.8 24.2 %all_to_all.20 = bf16[4,192,1024]{2,1,0:T(8,128)(2,1)} all-to-all(bf16[4,192,1024]{2,1,0:T(8,128)(2,1)S(1)} %bitcast.62), channel_id=1, replica_groups=mesh['dp'=2,'expert'=4,'tensor'=4] {'expert'}, dimensions={0} | all-to-all | bytes 3145728 | tf_op jit(solution)/shard_map/all_to_all | solution.py:45
  36.0 0.0 all-gather.4.cloned.1.call-update
  36.1 0.0 all-gather.6.cloned.1.call-start
  36.1 0.7 all-gather.6.cloned.1.call-update
  36.8 0.0 copy-start.2
  36.8 115.6 %all-gather.4.cloned.1.call-done = bf16[768,4096]{1,0:T(8,128)(2,1)} async-done(((bf16[768,1024]{1,0:T(8,128)(2,1)}), bf16[768,4096]{1,0:T(8,128)(2,1)}) %all-gather.4.cloned.1.call-update) | async-done | bytes 6291472 | tf_op jit(solution)/shard_map/all_gather | solution.py:50
  152.4 342.0 %all-gather.6.cloned.1.call-done = bf16[1,3584,4096]{2,1,0:T(8,128)(2,1)} async-done(((bf16[1,3584,2048]{2,1,0:T(8,128)(2,1)}), bf16[1,3584,4096]{2,1,0:T(8,128)(2,1)}) %all-gather.6.cloned.1.call-update) | async-done | bytes 29360144 | tf_op jit(solution)/shard_map/all_gather | solution.py:39
  494.4 34.1 %multiply_reduce_fusion = (f32[768]{0:T(1024)S(1)}, f32[768,3584]{1,0:T(8,128)}) fusion(bf16[1,768,3584]{2,1,0:T(8,128)(2,1)} %param.10, bf16[1,768,3584]{2,1,0:T(8,128)(2,1)} %param.9, bf16[768,4096]{1,0:T(8,128)(2,1)} %all-gather.4.cloned.1.call-done, bf16[1,3584,4096]{2,1,0:T(8,128)(2,1)} %all-gather.6.cloned.1.call-done), kind=kOutput, calls=%fused_computation.17 | convolution fusion | flops 22578855936 | bytes 57674752 | tf_op jit(solution)/shard_map/dot_general | solution.py:51
  528.4 0.1 all_to_all.15
  528.5 12.3 %psum.7 = f32[4,1,192]{2,1,0:T(1,128)} all-reduce(f32[4,1,192]{2,1,0:T(1,128)S(1)} %all_to_all.15), channel_id=1, replica_groups=mesh['dp'=2,'expert'=4,'tensor'=4] {'tensor'}, use_global_device_ids=true, to_apply=%region_6.7 | all-reduce | flops 768 | bytes 6144 | tf_op jit(solution)/shard_map/psum | solution.py:66
  540.8 3.2 all-to-all-start.2
  544.0 0.0 reduce-scatter.2.cloned.1.call-start
  544.1 0.0 copy-done.2
  544.1 3.7 all-to-all-done.2
  547.8 0.1 broadcast_in_dim.75
  547.9 0.5 select_reduce_fusion.1
  548.4 0.1 convert_element_type.92
  548.5 6.1 all_to_all.21
  554.6 0.1 reshape.73
  554.7 32.6 %convolution_convert_fusion = bf16[3584,4096]{1,0:T(8,128)(2,1)} fusion(bf16[768,4096]{1,0:T(8,128)(2,1)} %all-gather.4.cloned.1.call-done, f32[768]{0:T(1024)S(1)} %reshape.73, bf16[1,768,3584]{2,1,0:T(8,128)(2,1)} %param.10, bf16[1,768,3584]{2,1,0:T(8,128)(2,1)} %param.9), kind=kOutput, calls=%fused_computation | convolution fusion | flops 22594715648 | bytes 46664704 | tf_op jit(solution)/shard_map/dot_general | solution.py:55
  587.3 0.0 reduce-scatter.2.cloned.1.call-update
  587.3 0.6 pad_maximum_fusion
  587.9 0.0 copy-start.1
  587.9 15.9 %fusion.11 = (bf16[1,768,3584]{2,1,0:T(8,128)(2,1)}, bf16[1,768,3584]{2,1,0:T(8,128)(2,1)}) fusion(f32[768,3584]{1,0:T(8,128)} %get-tuple-element.14, f32[768]{0:T(1024)S(1)} %reshape.73, bf16[1,768,3584]{2,1,0:T(8,128)(2,1)} %param.9, bf16[1,768,3584]{2,1,0:T(8,128)(2,1)} %param.10), kind=kLoop, calls=%fused_computation.20 | loop fusion | flops 44040192 | bytes 33033216 | tf_op jit(solution)/shard_map/broadcast_in_dim | solution.py:82
  603.8 304.3 %reduce-scatter.2.cloned.1.call-done = bf16[3584,2048]{1,0:T(8,128)(2,1)} async-done(((bf16[3584,4096]{1,0:T(8,128)(2,1)}), bf16[3584,2048]{1,0:T(8,128)(2,1)}) %reduce-scatter.2.cloned.1.call-update) | async-done | bytes 14680080 | tf_op jit(solution)/shard_map/reduce_scatter | solution.py:59
  908.2 0.0 copy-done.1
  (6 shorter events, 0.1 us)
Async XLA Ops:
  7.2 3.9 copy-start
  7.2 145.2 %all-gather.4.cloned.1.call-start = ((), (), s32[]{:S(2)}) async-start(), calls=%async_computation.4 | async-start | bytes 7864320 | tf_op jit(solution)/shard_map/all_gather | solution.py:50
  36.1 458.3 %all-gather.6.cloned.1.call-start = ((), (), s32[]{:S(2)}) async-start(), calls=%async_computation.6 | async-start | bytes 44040192 | tf_op jit(solution)/shard_map/all_gather | solution.py:39
  36.8 507.3 %copy-start.2 = (bf16[256,2]{0,1:T(2,128)(2,1)S(1)}, bf16[256,2]{0,1:T(2,128)(2,1)}, u32[]{:S(2)}) copy-start(bf16[256,2]{0,1:T(2,128)(2,1)} %param.8) | copy-start | bytes 3076
  540.8 7.0 all-to-all-start.2
  544.0 364.1 %reduce-scatter.2.cloned.1.call-start = ((), (), s32[]{:S(2)}) async-start(), calls=%async_computation.5 | async-start | bytes 44040192 | tf_op jit(solution)/shard_map/reduce_scatter | solution.py:59
  587.9 320.3 %copy-start.1 = (bf16[256,1024]{1,0:T(8,128)(2,1)S(1)}, bf16[256,1024]{1,0:T(8,128)(2,1)}, u32[]{:S(2)}) copy-start(bf16[256,1024]{1,0:T(8,128)(2,1)} %param.6) | copy-start | bytes 1572868
Sparse Core Ops, SparseCore 0:
  36.2 116.1 all-gather.3
  153.9 340.3 all-gather.5
  587.4 320.6 reduce-scatter.1
where the time goes:
time: 915 us
  waiting for transfers between devices  766 us (84%)
  matrix products  67.4 us (7%)
  blocking collectives  42.6 us (5%)
  other arithmetic  19.3 us (2%)
  between operations  13.8 us (2%)
    all_gather x1, waiting for transfers between devices, local(): whole_weight = lax.all_gather(local_weight, 'dp', axis=1, tiled=True)  342 us
    reduce_scatter x1, waiting for transfers between devices, local(): lax.psum_scatter(rounded.astype(jnp.bfloat16), 'dp', scatter_dimension=1,...  304 us
    all_gather x1, waiting for transfers between devices, local(): fragment = lax.all_gather(narrow_rows, 'tensor', axis=1, tiled=True)  116 us
    dot_general x1, matrix products, local(): lax.dot_general(fragment, whole_weight, contract_cols, preferred_element_...  34.1 us
    dot_general x1, matrix products, local(): lax.dot_general(hidden, scaled, contract_rows, preferred_element_type=jnp...  32.6 us
    all_to_all x1, blocking collectives, local(): lax.all_to_all(outgoing, 'expert', split_axis=0, concat_axis=0, tiled=True)  24.2 us
  transfers between devices with their start and end apart: 4, of which 4 were waited for; matrix products, arithmetic and copies ran while one was open for 2% of the time, Pallas kernels for 0%

commit v1 on v0

--- a/solution.py
+++ b/solution.py
@@ -47,7 +47,13 @@
     )
     narrow_rows = received.reshape(expert_count * capacity, -1)
     gate_column = gate_slots.reshape(-1).astype(jnp.float32)[:, None]
-    fragment = lax.all_gather(narrow_rows, "tensor", axis=1, tiled=True)
+    count = lax.axis_size("tensor")
+    held, pieces = (narrow_rows, [narrow_rows])
+    for _ in range(count - 1):
+        held = lax.ppermute(held, "tensor", [(i, (i + 1) % count) for i in range(count)])
+        pieces.insert(0, held)
+    flat = jnp.concatenate(pieces, axis=1)
+    fragment = jnp.roll(flat, (lax.axis_index("tensor") + 1) * narrow_rows.shape[1], axis=1)
     upstream_sum = lax.dot_general(
         fragment, whole_weight, contract_cols, preferred_element_type=jnp.float32
     )

time: 915 us -> 776 us (0.85)
  waiting for transfers between devices: 766 us -> 608 us
  local copies, waits for them, and re-layouts: 1.92 us -> 19.5 us
    all_gather x1, waiting for transfers between devices: 342 us -> 190 us  [local(): whole_weight = lax.all_gather(local_weight, 'dp', axis=1, tiled=True)]
    all_gather x1 -> x0, waiting for transfers between devices: 116 us -> none  [local(): fragment = lax.all_gather(narrow_rows, 'tensor', axis=1, tiled=True)]
    ppermute x0 -> x3, waiting for transfers between devices: none -> 109 us  [local(): lax.ppermute(held, 'tensor', [(i, (i + 1) % count) for i in range(count)])]
    unnamed x7 -> x20, local copies, waits for them, and re-layouts: 0.88 us -> 17.2 us
  transfers between devices with their start and end apart: 4 -> 6, of which waited for: 4 -> 6; matrix products, arithmetic and copies ran while one was open for 2% -> 5% of each run, Pallas kernels for 0% -> 0%
where the time goes in v1:
time: 776 us; the launch traced here: 775 us
  waiting for transfers between devices  608 us (78%)
  matrix products  67.5 us (9%)
  blocking collectives  42.5 us (5%)
  local copies, waits for them, and re-layouts  19.5 us (3%)
  other arithmetic  18.6 us (2%)
  between operations  14.2 us (2%)
    reduce_scatter x1, waiting for transfers between devices, local(): lax.psum_scatter(rounded.astype(jnp.bfloat16), 'dp', scatter_dimension=1,...  304 us
    all_gather x1, waiting for transfers between devices, local(): whole_weight = lax.all_gather(local_weight, 'dp', axis=1, tiled=True)  190 us
    ppermute x3, waiting for transfers between devices, local(): lax.ppermute(held, 'tensor', [(i, (i + 1) % count) for i in range(count)])  109 us
    dot_general x1, matrix products, local(): lax.dot_general(fragment, whole_weight, contract_cols, preferred_element_...  34.1 us
    dot_general x1, matrix products, local(): lax.dot_general(hidden, scaled, contract_rows, preferred_element_type=jnp...  32.6 us
    all_to_all x1, blocking collectives, local(): lax.all_to_all(outgoing, 'expert', split_axis=0, concat_axis=0, tiled=True)  24.1 us
    unnamed x20, local copies, waits for them, and re-layouts  17.2 us
    broadcast_in_dim x1, other arithmetic, local(): return (gate_grad[None], up_grad[None], down_grad[None], router_grad)  15.9 us
  transfers between devices with their start and end apart: 6, of which 6 were waited for; matrix products, arithmetic and copies ran while one was open for 5% of the time, Pallas kernels for 0%

profile of v1, /device:TPU:0, one launch (start us, length us, event | category | flops | bytes accessed | tf_op | source)
XLA Modules:
  0.0 775.2 jit_solution(15555246217838544934)
XLA Ops:
  7.2 0.0 copy-start
  7.2 0.0 all-gather.3.cloned.1.call-start
  7.2 0.7 all-gather.3.cloned.1.call-update
  7.9 0.0 copy-done.4
  7.9 0.1 copy.28
  8.1 0.1 eq.62
  8.2 0.1 eq.58
  8.4 1.2 reduce-window.6
  9.6 0.2 slice_reduce_fusion
  9.8 0.2 reduce-window.9
  10.0 0.1 add_bitcast_fusion
  10.1 0.1 reduce_sum.48
  10.3 0.1 copy.30
  10.3 0.0 copy-done
  10.4 0.8 convolution_convert_fusion.1
  11.1 24.1 %all_to_all.20 = bf16[4,192,1024]{2,1,0:T(8,128)(2,1)S(1)} all-to-all(bf16[4,192,1024]{2,1,0:T(8,128)(2,1)S(1)} %bitcast.63), channel_id=1, replica_groups=mesh['dp'=2,'expert'=4,'tensor'=4] {'expert'}, dimensions={0} | all-to-all | bytes 3145728 | tf_op jit(solution)/shard_map/all_to_all | solution.py:45
  35.2 1.6 collective-permute-start
  36.8 36.1 %collective-permute-done = bf16[768,1024]{1,0:T(8,128)(2,1)S(1)} collective-permute-done((bf16[768,1024]{1,0:T(8,128)(2,1)S(1)}, bf16[768,1024]{1,0:T(8,128)(2,1)S(1)}, u32[]{:S(2)}, u32[]{:S(2)}) %collective-permute-start) | collective-permute-done | bytes 1572896 | tf_op jit(solution)/shard_map/ppermute | solution.py:53
  72.9 1.1 copy-done.2
  74.0 0.0 collective-permute-start.1
  74.0 36.8 %collective-permute-done.1 = bf16[768,1024]{1,0:T(8,128)(2,1)} collective-permute-done((bf16[768,1024]{1,0:T(8,128)(2,1)S(1)}, bf16[768,1024]{1,0:T(8,128)(2,1)}, u32[]{:S(2)}, u32[]{:S(2)}) %collective-permute-start.1) | collective-permute-done | bytes 1572896 | tf_op jit(solution)/shard_map/ppermute | solution.py:53
  110.8 0.0 collective-permute-start.2
  110.9 36.1 %collective-permute-done.2 = bf16[768,1024]{1,0:T(8,128)(2,1)} collective-permute-done((bf16[768,1024]{1,0:T(8,128)(2,1)}, bf16[768,1024]{1,0:T(8,128)(2,1)}, u32[]{:S(2)}, u32[]{:S(2)}) %collective-permute-start.2) | collective-permute-done | bytes 1572896 | tf_op jit(solution)/shard_map/ppermute | solution.py:53
  147.0 2.7 constant_dynamic-update-slice_fusion.7
  149.6 2.7 constant_dynamic-update-slice_fusion.6
  152.3 2.7 constant_dynamic-update-slice_fusion.5
  155.0 1.3 constant_dynamic-update-slice_fusion.4
  156.2 2.7 constant_dynamic-update-slice_fusion.3
  158.9 2.7 constant_dynamic-update-slice_fusion.2
  161.6 1.3 constant_dynamic-update-slice_fusion.1
  162.8 1.3 constant_dynamic-update-slice_fusion
  164.1 190.5 %all-gather.3.cloned.1.call-done = bf16[1,3584,4096]{2,1,0:T(8,128)(2,1)} async-done(((bf16[1,3584,2048]{2,1,0:T(8,128)(2,1)}), bf16[1,3584,4096]{2,1,0:T(8,128)(2,1)}) %all-gather.3.cloned.1.call-update) | async-done | bytes 29360144 | tf_op jit(solution)/shard_map/all_gather | solution.py:39
  354.5 34.1 %multiply_reduce_fusion = (f32[768]{0:T(1024)S(1)}, f32[768,3584]{1,0:T(8,128)}) fusion(bf16[1,768,3584]{2,1,0:T(8,128)(2,1)} %param.10, bf16[1,768,3584]{2,1,0:T(8,128)(2,1)} %param.9, bf16[1,3584,4096]{2,1,0:T(8,128)(2,1)} %all-gather.3.cloned.1.call-done, bf16[768,8192]{1,0:T(8,128)(2,1)} %constant_dynamic-update-slice_fusion, s32[]{:T(128)S(6)} %select_n.39), kind=kOutput, calls=%fused_computation.17 | convolution fusion | flops 22578855936 | bytes 57674756 | tf_op jit(solution)/shard_map/dot_general | solution.py:57
  388.6 0.1 all_to_all.15
  388.7 12.2 %psum.7 = f32[4,1,192]{2,1,0:T(1,128)} all-reduce(f32[4,1,192]{2,1,0:T(1,128)S(1)} %all_to_all.15), channel_id=1, replica_groups=mesh['dp'=2,'expert'=4,'tensor'=4] {'tensor'}, use_global_device_ids=true, to_apply=%region_6.7 | all-reduce | flops 768 | bytes 6144 | tf_op jit(solution)/shard_map/psum | solution.py:72
  400.9 3.2 all-to-all-start.2
  404.2 0.0 reduce-scatter.2.cloned.1.call-start
  404.3 3.7 all-to-all-done.2
  408.0 0.1 broadcast_in_dim.75
  408.1 0.5 select_reduce_fusion.1
  408.5 0.1 convert_element_type.92
  408.6 6.1 all_to_all.21
  414.8 0.1 reshape.73
  414.9 32.6 %convolution_convert_fusion = bf16[3584,4096]{1,0:T(8,128)(2,1)} fusion(f32[768]{0:T(1024)S(1)} %reshape.73, bf16[768,8192]{1,0:T(8,128)(2,1)} %constant_dynamic-update-slice_fusion, s32[]{:T(128)S(6)} %select_n.39, bf16[1,768,3584]{2,1,0:T(8,128)(2,1)} %param.10, bf16[1,768,3584]{2,1,0:T(8,128)(2,1)} %param.9), kind=kOutput, calls=%fused_computation | convolution fusion | flops 22594715648 | bytes 46664708 | tf_op jit(solution)/shard_map/dot_general | solution.py:61
  447.5 0.0 reduce-scatter.2.cloned.1.call-update
  447.5 0.6 pad_maximum_fusion
  448.1 15.9 %fusion.13 = (bf16[1,768,3584]{2,1,0:T(8,128)(2,1)}, bf16[1,768,3584]{2,1,0:T(8,128)(2,1)}) fusion(f32[768,3584]{1,0:T(8,128)} %get-tuple-element.14, f32[768]{0:T(1024)S(1)} %reshape.73, bf16[1,768,3584]{2,1,0:T(8,128)(2,1)} %param.9, bf16[1,768,3584]{2,1,0:T(8,128)(2,1)} %param.10), kind=kLoop, calls=%fused_computation.22 | loop fusion | flops 44040192 | bytes 33033216 | tf_op jit(solution)/shard_map/broadcast_in_dim | solution.py:88
  464.0 304.3 %reduce-scatter.2.cloned.1.call-done = bf16[3584,2048]{1,0:T(8,128)(2,1)} async-done(((bf16[3584,4096]{1,0:T(8,128)(2,1)}), bf16[3584,2048]{1,0:T(8,128)(2,1)}) %reduce-scatter.2.cloned.1.call-update) | async-done | bytes 14680080 | tf_op jit(solution)/shard_map/reduce_scatter | solution.py:65
  (15 shorter events, 0.1 us)
Async XLA Ops:
  7.2 3.2 copy-start
  7.2 0.7 copy-start.4
  7.2 347.4 %all-gather.3.cloned.1.call-start = ((), (), s32[]{:S(2)}) async-start(), calls=%async_computation.5 | async-start | bytes 44040192 | tf_op jit(solution)/shard_map/all_gather | solution.py:39
  35.2 37.6 %collective-permute-start = (bf16[768,1024]{1,0:T(8,128)(2,1)S(1)}, bf16[768,1024]{1,0:T(8,128)(2,1)S(1)}, u32[]{:S(2)}, u32[]{:S(2)}) collective-permute-start(bf16[768,1024]{1,0:T(8,128)(2,1)S(1)} %bitcast.60), channel_id=1, source_target_pairs={{0,1},{1,2},{2,3},{3,0},{4,5},{5,6},{6,7},{7,4},{8,9},{9,10},{10,1... | collective-permute-start | bytes 4718600 | tf_op jit(solution)/shard_map/ppermute | solution.py:53
  72.9 1.1 copy-start.2
  74.0 36.8 %collective-permute-start.1 = (bf16[768,1024]{1,0:T(8,128)(2,1)S(1)}, bf16[768,1024]{1,0:T(8,128)(2,1)}, u32[]{:S(2)}, u32[]{:S(2)}) collective-permute-start(bf16[768,1024]{1,0:T(8,128)(2,1)S(1)} %collective-permute-done), channel_id=1, source_target_pairs={{0,1},{1,2},{2,3},{3,0},{4,5},{5,6},{6,7},{7,4},{8,9},{9,10},{10,1... | collective-permute-start | bytes 4718600 | tf_op jit(solution)/shard_map/ppermute | solution.py:53
  110.8 36.1 %collective-permute-start.2 = (bf16[768,1024]{1,0:T(8,128)(2,1)}, bf16[768,1024]{1,0:T(8,128)(2,1)}, u32[]{:S(2)}, u32[]{:S(2)}) collective-permute-start(bf16[768,1024]{1,0:T(8,128)(2,1)} %collective-permute-done.1), channel_id=1, source_target_pairs={{0,1},{1,2},{2,3},{3,0},{4,5},{5,6},{6,7},{7,4},{8,9},{9,10},{10,1... | collective-permute-start | bytes 4718600 | tf_op jit(solution)/shard_map/ppermute | solution.py:53
  110.8 50.7 %copy-start.3 = (bf16[768,1024]{1,0:T(8,128)(2,1)S(1)}, bf16[768,1024]{1,0:T(8,128)(2,1)}, u32[]{:S(2)}) copy-start(bf16[768,1024]{1,0:T(8,128)(2,1)} %copy-done.2) | copy-start | bytes 4718596
  164.1 240.2 %copy-start.5 = (bf16[256,2]{0,1:T(2,128)(2,1)S(1)}, bf16[256,2]{0,1:T(2,128)(2,1)}, u32[]{:S(2)}) copy-start(bf16[256,2]{0,1:T(2,128)(2,1)} %param.8) | copy-start | bytes 3076
  400.9 7.0 all-to-all-start.2
  404.2 364.1 %reduce-scatter.2.cloned.1.call-start = ((), (), s32[]{:S(2)}) async-start(), calls=%async_computation.4 | async-start | bytes 44040192 | tf_op jit(solution)/shard_map/reduce_scatter | solution.py:65
  448.1 320.3 %copy-start.1 = (bf16[256,1024]{1,0:T(8,128)(2,1)S(1)}, bf16[256,1024]{1,0:T(8,128)(2,1)}, u32[]{:S(2)}) copy-start(bf16[256,1024]{1,0:T(8,128)(2,1)} %param.6) | copy-start | bytes 1572868
Sparse Core Ops, SparseCore 0:
  9.6 344.9 all-gather.2
  447.6 320.6 reduce-scatter.1
